TPU v7x, 32 devices: a whole 2x2x4 slice. The times are simulated.
32 devices in a mesh: fsdp: 4 (over x, core), replica: 8 (over z, y).
Axes of the slice: x: 2, y: 2, z: 4, core: 2. Of those that a mesh axis runs over, the one named last changes fastest.
Arguments:
- hidden_in: bfloat16 [16384, 768], P(('fsdp', 'replica')), may hold values from -6 to 6
- encoder_states: bfloat16 [16384, 768], P(('fsdp', 'replica')), may hold values from -6 to 6
- output_grad: bfloat16 [16384, 768], P(('fsdp', 'replica')), may hold values from -6 to 6
- piece_starts: int32 [32, 3], P(('fsdp', 'replica')), may hold values from 0 to 384, as said below
- selfquery: bfloat16 [768, 768], P('fsdp'), may hold values from -0.0546875 to 0.0546875
- selfkey: bfloat16 [768, 768], P('fsdp'), may hold values from -0.21875 to 0.21875
- selfvalue: bfloat16 [768, 768], P('fsdp'), may hold values from -0.21875 to 0.21875
- selfproj: bfloat16 [768, 768], P('fsdp'), may hold values from -0.875 to 0.875
- crossquery: bfloat16 [768, 768], P('fsdp'), may hold values from -0.0546875 to 0.0546875
- crosskey: bfloat16 [768, 768], P('fsdp'), may hold values from -0.21875 to 0.21875
- crossvalue: bfloat16 [768, 768], P('fsdp'), may hold values from -0.21875 to 0.21875
- crossproj: bfloat16 [768, 768], P('fsdp'), may hold values from -0.875 to 0.875
- gateproj: bfloat16 [768, 2048], P('fsdp'), may hold values from -0.21875 to 0.21875
- upproj: bfloat16 [768, 2048], P('fsdp'), may hold values from -0.21875 to 0.21875
- downproj: bfloat16 [2048, 768], P('fsdp'), may hold values from -0.125 to 0.125
- gainself: bfloat16 [768], P('fsdp'), may hold values from 0.5 to 1.5
- gaincross: bfloat16 [768], P('fsdp'), may hold values from 0.5 to 1.5
- gainffn: bfloat16 [768], P('fsdp'), may hold values from 0.5 to 1.5
- reltable: bfloat16 [32, 12], P('fsdp'), may hold values from -4 to 4
Outputs:
- layer_out: bfloat16 [16384, 768], P(('fsdp', 'replica'))
- hidden_grad: float32 [16384, 768], P(('fsdp', 'replica'))
- encoder_grad: float32 [16384, 768], P(('fsdp', 'replica'))
- selfquery_grad: float32 [768, 768], P('fsdp')
- selfkey_grad: float32 [768, 768], P('fsdp')
- selfvalue_grad: float32 [768, 768], P('fsdp')
- selfproj_grad: float32 [768, 768], P('fsdp')
- crossquery_grad: float32 [768, 768], P('fsdp')
- crosskey_grad: float32 [768, 768], P('fsdp')
- crossvalue_grad: float32 [768, 768], P('fsdp')
- crossproj_grad: float32 [768, 768], P('fsdp')
- gateproj_grad: float32 [768, 2048], P('fsdp')
- upproj_grad: float32 [768, 2048], P('fsdp')
- downproj_grad: float32 [2048, 768], P('fsdp')
- gainself_grad: float32 [768], P('fsdp')
- gaincross_grad: float32 [768], P('fsdp')
- gainffn_grad: float32 [768], P('fsdp')
- reltable_grad: float32 [32, 12], P('fsdp')
Inputs may be any that keep to these rules, and one draw needn't show every extreme that they name: `piece_starts`: each row holds the 3 increasing starts of one sequence's pieces, the first 0 and the last exactly 384; no piece has more than 256 tokens, and each sequence has one piece of exactly 256.
All inputs are finite; a program needn't handle non-finite values.
Results may differ from a plain program's by a relative error of at most 0.028.
The roundings to bfloat16 on the way count: a program that leaves them out, or rounds other values in their place, can miss the bound.
Values may be sent and summed in bfloat16 or wider, within the bound.
No kernel may reach another device: no remote copies, remote signals or barrier semaphores. Data moves between devices by JAX's collectives and lax.ppermute only.
A program may use at most 256 MiB of HBM per device.

v0:
```python
import jax
import jax.numpy as jnp
from jax import lax
from jax.sharding import PartitionSpec as P

HEADS = 12
HEAD_DIM = 64
BUCKETS = 32
QBLOCK = 512
EPS = 1e-06
NEG = -1000000000.0
EDGES = (1, 2, 3, 4, 5, 6, 7, 8, 12, 16, 23, 32, 46, 64, 91)


def rms_scale(hidden, gain):
    return hidden * lax.rsqrt(jnp.mean(hidden * hidden, axis=-1, keepdims=True) + EPS) * gain


def gated(gate, upper):
    return jax.nn.gelu(gate, approximate=True) * upper


def product(left, right):
    return jnp.dot(left, right, preferred_element_type=jnp.float32)


def left_product(left, right):
    return lax.dot_general(
        left, right, (((0,), (0,)), ((), ())), preferred_element_type=jnp.float32
    )


def right_product(left, right):
    return lax.dot_general(
        left, right, (((1,), (1,)), ((), ())), preferred_element_type=jnp.float32
    )


def split_heads(matrix):
    return matrix.reshape(matrix.shape[0], HEADS, HEAD_DIM)


def block_terms(context, block_rows, key_count):
    if context is None:
        return (None, None, None)
    rel_table, piece_ids = context
    query_pos = jnp.arange(block_rows, dtype=jnp.int32)
    key_pos = jnp.arange(key_count, dtype=jnp.int32)
    relative = key_pos[None, :] - query_pos[:, None]
    distance = jnp.abs(relative)
    bucket = 16 * (relative > 0).astype(jnp.int32)
    for edge_len in EDGES:
        bucket = bucket + (distance >= edge_len).astype(jnp.int32)
    onehot = (bucket[:, :, None] == jnp.arange(BUCKETS, dtype=jnp.int32)[None, None, :]).astype(
        jnp.bfloat16
    )
    bias_block = jnp.einsum("qkb,bh->hqk", onehot, rel_table, preferred_element_type=jnp.float32)
    allowed = (key_pos[None, :] <= query_pos[:, None]) | (piece_ids[None, :] == piece_ids[:, None])
    return (onehot, bias_block, allowed)


def block_scores(query_block, key_heads, bias_block, allowed):
    scores = jnp.einsum("qhd,khd->hqk", query_block, key_heads, preferred_element_type=jnp.float32)
    if bias_block is not None:
        scores = jnp.where(allowed[None], scores + bias_block, NEG)
    return scores


def attend_forward(queries, key_rows, value_rows, context):
    key_heads = split_heads(key_rows)
    value_heads = split_heads(value_rows)
    query_block = split_heads(queries)
    onehot, bias_block, allowed = block_terms(context, QBLOCK, key_rows.shape[0])
    scores = block_scores(query_block, key_heads, bias_block, allowed)
    row_max = jnp.max(scores, axis=-1, keepdims=True)
    raised = jnp.exp(scores - row_max)
    row_sum = jnp.sum(raised, axis=-1, keepdims=True)
    prob_low = (raised / row_sum).astype(jnp.bfloat16)
    mixed_block = jnp.einsum(
        "hqk,khd->qhd", prob_low, value_heads, preferred_element_type=jnp.float32
    )
    mixed_parts = mixed_block.reshape(QBLOCK, HEADS * HEAD_DIM).astype(jnp.bfloat16)
    lse_parts = row_max + jnp.log(row_sum)
    return (mixed_parts, lse_parts)


def attend_backward(queries, key_rows, value_rows, grad_mixed, lse_rows, context):
    key_count = key_rows.shape[0]
    key_heads = split_heads(key_rows)
    value_heads = split_heads(value_rows)
    table_grad = jnp.zeros((BUCKETS, HEADS), jnp.float32)
    query_block = split_heads(queries)
    grad_block = split_heads(grad_mixed)
    onehot, bias_block, allowed = block_terms(context, QBLOCK, key_count)
    scores = block_scores(query_block, key_heads, bias_block, allowed)
    probs = jnp.exp(scores - lse_rows)
    prob_low = probs.astype(jnp.bfloat16)
    grad_probs = jnp.einsum(
        "qhd,khd->hqk", grad_block, value_heads, preferred_element_type=jnp.float32
    )
    inner_sum = jnp.sum(probs * grad_probs, axis=-1, keepdims=True)
    grad_scores = (probs * (grad_probs - inner_sum)).astype(jnp.bfloat16)
    query_grad = jnp.einsum(
        "hqk,khd->qhd", grad_scores, key_heads, preferred_element_type=jnp.float32
    )
    query_parts = query_grad.reshape(QBLOCK, HEADS * HEAD_DIM).astype(jnp.bfloat16)
    key_grad = jnp.einsum(
        "hqk,qhd->khd", grad_scores, query_block, preferred_element_type=jnp.float32
    )
    value_grad = jnp.einsum(
        "hqk,qhd->khd", prob_low, grad_block, preferred_element_type=jnp.float32
    )
    if onehot is not None:
        table_grad = jnp.einsum(
            "hqk,qkb->bh", grad_scores, onehot, preferred_element_type=jnp.float32
        )
    key_low = key_grad.reshape(key_count, HEADS * HEAD_DIM).astype(jnp.bfloat16)
    value_low = value_grad.reshape(key_count, HEADS * HEAD_DIM).astype(jnp.bfloat16)
    return (query_parts, key_low, value_low, table_grad)


def make_on_device(fsdp_size, replica_size):

    def on_device(
        hidden_in,
        encoder_states,
        output_grad,
        piece_starts,
        selfquery,
        selfkey,
        selfvalue,
        selfproj,
        crossquery,
        crosskey,
        crossvalue,
        crossproj,
        gateproj,
        upproj,
        downproj,
        gainself,
        gaincross,
        gainffn,
        reltable,
    ):
        shard_rows, width = selfquery.shape
        ff_width = gateproj.shape[1]
        table_rows = reltable.shape[0]
        self_packed = jnp.concatenate([selfquery, selfkey, selfvalue], axis=1)
        small_packed = jnp.concatenate([gainself, gaincross, gainffn, reltable.reshape(-1)])
        mid_packed = jnp.concatenate(
            [selfproj, crossquery, crosskey, crossvalue, crossproj], axis=1
        )
        ffn_packed = jnp.concatenate([gateproj, upproj, downproj.reshape(shard_rows, -1)], axis=1)
        self_full = lax.all_gather(self_packed, "fsdp", axis=0, tiled=True)
        small_full = lax.all_gather(small_packed, "fsdp", axis=0, tiled=False)
        mid_full = lax.all_gather(mid_packed, "fsdp", axis=0, tiled=True)
        ffn_full = lax.all_gather(ffn_packed, "fsdp", axis=0, tiled=True)
        gain_one = small_full[:, 0:shard_rows].reshape(-1)
        gain_two = small_full[:, shard_rows : 2 * shard_rows].reshape(-1)
        gain_three = small_full[:, 2 * shard_rows : 3 * shard_rows].reshape(-1)
        table_full = small_full[:, 3 * shard_rows :].reshape(-1, HEADS)
        self_proj = mid_full[:, 0:width]
        cross_query = mid_full[:, width : 2 * width]
        cross_kv = mid_full[:, 2 * width : 4 * width]
        cross_key = cross_kv[:, :width]
        cross_value = cross_kv[:, width:]
        cross_proj = mid_full[:, 4 * width : 5 * width]
        gate_up = ffn_full[:, : 2 * ff_width]
        down_full = (
            ffn_full[:, 2 * ff_width :]
            .reshape(fsdp_size, shard_rows, ff_width)
            .reshape(ff_width, width)
        )
        length = hidden_in.shape[0]
        position = jnp.arange(length, dtype=jnp.int32)
        piece_ids = (
            jnp.sum((piece_starts[0][None, :] <= position[:, None]).astype(jnp.int32), axis=1) - 1
        )
        context = (table_full, piece_ids)
        resid_in = hidden_in.astype(jnp.float32)
        normed_one = rms_scale(resid_in, gain_one.astype(jnp.float32)).astype(jnp.bfloat16)
        qkv_one = product(normed_one, self_full).astype(jnp.bfloat16)
        query_one = qkv_one[:, :width]
        key_one = qkv_one[:, width : 2 * width]
        value_one = qkv_one[:, 2 * width :]
        mixed_one, lse_one = attend_forward(query_one, key_one, value_one, context)
        after_self = resid_in + product(mixed_one, self_proj)
        normed_two = rms_scale(after_self, gain_two.astype(jnp.float32)).astype(jnp.bfloat16)
        query_two = product(normed_two, cross_query).astype(jnp.bfloat16)
        kv_two = product(encoder_states, cross_kv).astype(jnp.bfloat16)
        key_two = kv_two[:, :width]
        value_two = kv_two[:, width:]
        mixed_two, lse_two = attend_forward(query_two, key_two, value_two, None)
        after_cross = after_self + product(mixed_two, cross_proj)
        normed_three = rms_scale(after_cross, gain_three.astype(jnp.float32)).astype(jnp.bfloat16)
        gate_upper = product(normed_three, gate_up)
        gate_pre = gate_upper[:, :ff_width]
        upper_pre = gate_upper[:, ff_width:]
        inner = gated(gate_pre, upper_pre).astype(jnp.bfloat16)
        layer_out = (after_cross + product(inner, down_full)).astype(jnp.bfloat16)

        def reduce_rows(packed):
            owned = lax.psum_scatter(
                packed.astype(jnp.bfloat16), ("fsdp", "replica"), scatter_dimension=0, tiled=True
            )
            return lax.all_gather(owned, "replica", axis=0, tiled=True)

        downproj_grad = left_product(inner, output_grad)
        inner_grad = right_product(output_grad, down_full)
        gated_value, pull_gate = jax.vjp(gated, gate_pre, upper_pre)
        gate_grad, upper_grad = pull_gate(inner_grad)
        gate_upper_low = jnp.concatenate(
            [gate_grad.astype(jnp.bfloat16), upper_grad.astype(jnp.bfloat16)], axis=1
        )
        gate_up_grad = left_product(normed_three, gate_upper_low)
        ffn_owned = reduce_rows(
            jnp.concatenate([gate_up_grad, downproj_grad.reshape(width, ff_width)], axis=1)
        )
        normed_grad = right_product(gate_upper_low, gate_up)
        norm_value, pull_norm = jax.vjp(rms_scale, after_cross, gain_three.astype(jnp.float32))
        back_resid, gainffn_grad = pull_norm(normed_grad)
        resid_grad = output_grad.astype(jnp.float32) + back_resid
        branch_low = resid_grad.astype(jnp.bfloat16)
        crossproj_grad = left_product(mixed_two, branch_low)
        mixed_grad = right_product(branch_low, cross_proj).astype(jnp.bfloat16)
        query_back, key_back, value_back, unused_table = attend_backward(
            query_two, key_two, value_two, mixed_grad, lse_two, None
        )
        crossquery_grad = left_product(normed_two, query_back)
        kv_back = jnp.concatenate([key_back, value_back], axis=1)
        crosskv_grad = left_product(encoder_states, kv_back)
        cross_owned = reduce_rows(
            jnp.concatenate([crossproj_grad, crossquery_grad, crosskv_grad], axis=1)
        )
        encoder_grad = right_product(kv_back, cross_kv)
        normed_grad = right_product(query_back, cross_query)
        norm_value, pull_norm = jax.vjp(rms_scale, after_self, gain_two.astype(jnp.float32))
        back_resid, gaincross_grad = pull_norm(normed_grad)
        resid_grad = resid_grad + back_resid
        branch_low = resid_grad.astype(jnp.bfloat16)
        selfproj_grad = left_product(mixed_one, branch_low)
        mixed_grad = right_product(branch_low, self_proj).astype(jnp.bfloat16)
        query_back, key_back, value_back, reltable_grad = attend_backward(
            query_one, key_one, value_one, mixed_grad, lse_one, context
        )
        qkv_back = jnp.concatenate([query_back, key_back, value_back], axis=1)
        selfqkv_grad = left_product(normed_one, qkv_back)
        self_owned = reduce_rows(jnp.concatenate([selfproj_grad, selfqkv_grad], axis=1))
        normed_grad = right_product(qkv_back, self_full)
        norm_value, pull_norm = jax.vjp(rms_scale, resid_in, gain_one.astype(jnp.float32))
        back_resid, gainself_grad = pull_norm(normed_grad)
        hidden_grad = resid_grad + back_resid
        small_sum = lax.psum(
            jnp.concatenate(
                [gainself_grad, gaincross_grad, gainffn_grad, reltable_grad.reshape(-1)]
            ),
            ("fsdp", "replica"),
        )
        me = lax.axis_index("fsdp")
        gain_block = lambda i: lax.dynamic_slice_in_dim(
            small_sum, i * width + me * shard_rows, shard_rows
        )
        table_block = lax.dynamic_slice_in_dim(
            small_sum[3 * width :].reshape(-1, HEADS), me * table_rows, table_rows
        )
        as_f32 = lambda v: v.astype(jnp.float32)
        return (
            layer_out,
            hidden_grad,
            encoder_grad,
            as_f32(self_owned[:, width : 2 * width]),
            as_f32(self_owned[:, 2 * width : 3 * width]),
            as_f32(self_owned[:, 3 * width : 4 * width]),
            as_f32(self_owned[:, 0:width]),
            as_f32(cross_owned[:, width : 2 * width]),
            as_f32(cross_owned[:, 2 * width : 3 * width]),
            as_f32(cross_owned[:, 3 * width : 4 * width]),
            as_f32(cross_owned[:, 0:width]),
            as_f32(ffn_owned[:, 0:ff_width]),
            as_f32(ffn_owned[:, ff_width : 2 * ff_width]),
            as_f32(ffn_owned[:, 2 * ff_width :].reshape(-1, width)),
            gain_block(0),
            gain_block(1),
            gain_block(2),
            table_block,
        )

    return on_device


def solution(mesh):
    placed = (
        P(("fsdp", "replica"), None),
        P(("fsdp", "replica"), None),
        P(("fsdp", "replica"), None),
        P(("fsdp", "replica"), None),
        P("fsdp", None),
        P("fsdp", None),
        P("fsdp", None),
        P("fsdp", None),
        P("fsdp", None),
        P("fsdp", None),
        P("fsdp", None),
        P("fsdp", None),
        P("fsdp", None),
        P("fsdp", None),
        P("fsdp", None),
        P("fsdp"),
        P("fsdp"),
        P("fsdp"),
        P("fsdp", None),
    )
    return jax.shard_map(
        make_on_device(mesh.shape["fsdp"], mesh.shape["replica"]),
        mesh=mesh,
        in_specs=placed,
        out_specs=(
            P(("fsdp", "replica"), None),
            P(("fsdp", "replica"), None),
            P(("fsdp", "replica"), None),
            P("fsdp", None),
            P("fsdp", None),
            P("fsdp", None),
            P("fsdp", None),
            P("fsdp", None),
            P("fsdp", None),
            P("fsdp", None),
            P("fsdp", None),
            P("fsdp", None),
            P("fsdp", None),
            P("fsdp", None),
            P("fsdp"),
            P("fsdp"),
            P("fsdp"),
            P("fsdp", None),
        ),
        check_vma=False,
    )
```

profile of v0, /device:TPU:0, one launch (start us, length us, event | category | flops | bytes accessed | tf_op | source)
XLA Modules:
  0.0 753.6 jit_solution(3771571763767273229)
XLA Ops:
  21.4 9.3 %all-reduce = bf16[2688]{0:T(1024)(128)(2,1)S(1)} all-reduce(bf16[2688]{0:T(1024)(128)(2,1)S(1)} %dynamic-update-slice), channel_id=2, replica_groups=mesh['fsdp'=4,'replica'=8] {'fsdp'}, use_global_device_ids=true, to_apply=%add | all-reduce | flops 2688 | bytes 10752
  31.9 8.7 %iota_compare_fusion = pred[512,512,32]{0,2,1:T(32,128)(4,1)} fusion(s32[512,512]{0,1:T(8,128)S(1)} %convert_add_fusion.1), kind=kLoop, calls=%fused_computation | loop fusion | flops 8388608 | bytes 9437184 | tf_op jit(solution)/shard_map/eq | solution.py:54
  40.5 46.2 %copy.117 = pred[512,512,32]{1,2,0:T(32,128)(4,1)S(1)} copy(pred[512,512,32]{0,2,1:T(32,128)(4,1)} %iota_compare_fusion) | data formatting | bytes 16777216 | tf_op jit(solution)/shard_map/eq | solution.py:54
  86.8 7.7 %fusion.83 = f32[12,512,512]{2,0,1:T(8,128)} fusion(pred[512,512,32]{1,2,0:T(32,128)(4,1)S(1)} %copy.117, bf16[32,12]{1,0:T(8,128)(2,1)S(1)} %reshape.325), kind=kOutput, calls=%fused_computation.155 | convolution fusion | flops 201326592 | bytes 20972288 | tf_op jit(solution)/shard_map/qkb,bh->hqk/dot_general | solution.py:57
  94.5 18.3 %copy.118 = f32[12,512,512]{1,2,0:T(8,128)} copy(f32[12,512,512]{2,0,1:T(8,128)} %fusion.83) | data formatting | bytes 25165824 | tf_op jit(solution)/shard_map/qkb,bh->hqk/dot_general | solution.py:57
  121.1 6.6 fusion.97
  165.8 6.6 reshape_reshape.3
  172.4 10.2 %fusion.16 = f32[512,4096]{1,0:T(8,128)} fusion(bf16[768,6144]{1,0:T(8,128)(2,1)} %all-gather.12.cloned.1.call-done, f32[512,768]{1,0:T(8,128)} %get-tuple-element.92, f32[768]{0:T(1024)S(1)} %reshape.337, f32[512]{0:T(512)S(1)} %fusion.87), kind=kOutput, calls=%fused_computation.30 | convolution fusion | flops 3222405120 | bytes 16258048 | tf_op jit(solution)/shard_map/dot_general | solution.py:24
  182.7 8.4 %fusion.24 = (bf16[512,2048]{1,0:T(8,128)(2,1)S(1)}, bf16[512,2048]{1,0:T(8,128)(2,1)S(1)}, bf16[512,2048]{1,0:T(8,128)(2,1)}) fusion(f32[512,4096]{1,0:T(8,128)} %fusion.16, bf16[2048,768]{1,0:T(8,128)(2,1)S(1)} %copy-done.28, bf16[512,768]{1,0:T(8,128)(2,1)S(1)} %copy-done.42), kind=kOutput, calls=%fused_computation.42 | convolution fusion | flops 1637875712 | bytes 18612224 | tf_op jit(solution)/shard_map/dot_general | solution.py:34
  203.2 7.9 %fusion.40 = bf16[12,64,512]{2,1,0:T(8,128)(2,1)} fusion(bf16[512,12,64]{0,2,1:T(8,128)(2,1)} %bitcast.98, f32[12,512,512]{1,2,0:T(8,128)} %copy-done.2, f32[12,512]{1,0:T(8,128)S(1)} %log_add_fusion.1), kind=kOutput, calls=%fused_computation.93 | convolution fusion | flops 409337856 | bytes 14180352 | tf_op jit(solution)/shard_map/hqk,qhd->khd/dot_general | solution.py:110
  211.1 9.0 %multiply_reduce_fusion.1 = (f32[12,512]{1,0:T(8,128)S(1)}, f32[12,512,512]{1,2,0:T(8,128)}) fusion(f32[12,512,512]{1,2,0:T(8,128)} %copy-done.2, f32[12,512]{1,0:T(8,128)S(1)} %log_add_fusion.1, bf16[512,12,64]{0,2,1:T(8,128)(2,1)S(1)} %bitcast.99, bf16[512,12,64]{0,2,1:T(8,128)(2,1)S(1)} %bitcast.109), kind=kOutput, calls=%fused_computation.5 | convolution fusion | flops 412084224 | bytes 26787840 | tf_op jit(solution)/shard_map/qhd,khd->hqk/dot_general | solution.py:98
  220.1 7.4 multiply_convert_fusion.1
  235.9 6.6 copy.148
  257.0 12.8 %multiply_reduce_fusion = (f32[12,512]{1,0:T(8,128)S(1)}, f32[12,512,512]{1,2,0:T(8,128)}) fusion(f32[12,512,512]{1,2,0:T(8,128)} %copy-done.1, f32[12,512]{1,0:T(8,128)S(1)} %log_add_fusion, bf16[512,12,64]{0,2,1:T(8,128)(2,1)} %bitcast.96, bf16[512,12,64]{0,2,1:T(8,128)(2,1)} %bitcast.107), kind=kOutput, calls=%fused_computation.2 | convolution fusion | flops 412084224 | bytes 26787840 | tf_op jit(solution)/shard_map/qhd,khd->hqk/dot_general | solution.py:98
  269.8 7.1 multiply_convert_fusion
  294.4 6.6 reshape.332
  301.0 6.4 convolution_convert_fusion
  311.7 39.2 %reduce-scatter.10.cloned.1.call-done = bf16[24,3072]{1,0:T(8,128)(2,1)} async-done(((bf16[768,3072]{1,0:T(8,128)(2,1)}), bf16[24,3072]{1,0:T(8,128)(2,1)}) %reduce-scatter.10.cloned.1.call-update) | async-done | bytes 147472 | tf_op jit(solution)/shard_map/reduce_scatter | solution.py:203
  351.0 111.8 %reduce-scatter.6.cloned.1.call-done = bf16[24,3072]{1,0:T(8,128)(2,1)} async-done(((bf16[768,3072]{1,0:T(8,128)(2,1)}), bf16[24,3072]{1,0:T(8,128)(2,1)}) %reduce-scatter.6.cloned.1.call-update) | async-done | bytes 147472 | tf_op jit(solution)/shard_map/reduce_scatter | solution.py:203
  462.8 141.1 %reduce-scatter.8.cloned.1.call-done = bf16[24,6144]{1,0:T(8,128)(2,1)} async-done(((bf16[768,6144]{1,0:T(8,128)(2,1)}), bf16[24,6144]{1,0:T(8,128)(2,1)}) %reduce-scatter.8.cloned.1.call-update) | async-done | bytes 294928 | tf_op jit(solution)/shard_map/reduce_scatter | solution.py:203
  604.0 8.5 %fusion.48 = f32[32,12]{1,0:T(8,128)S(1)} fusion(bf16[12,512,512]{1,2,0:T(8,128)(2,1)} %copy-done.3, s32[512,512]{0,1:T(8,128)S(1)} %copy-done.22), kind=kOutput, calls=%fused_computation.101 | convolution fusion | flops 209715200 | bytes 7341568 | tf_op jit(solution)/shard_map/hqk,qkb->bh/dot_general | solution.py:114
  619.0 40.8 %psum.7 = f32[2688]{0:T(1024)S(1)} all-reduce(f32[2688]{0:T(1024)S(1)} %pad_maximum_fusion.14), channel_id=1, replica_groups=mesh['fsdp'=4,'replica'=8] {'fsdp','replica'}, use_global_device_ids=true, to_apply=%region_19.20 | all-reduce | flops 2688 | bytes 21504 | tf_op jit(solution)/shard_map/psum | solution.py:253
  674.0 14.6 %all-gather.14.cloned.1.call-done = bf16[192,3072]{1,0:T(8,128)(2,1)} async-done(((bf16[24,3072]{1,0:T(8,128)(2,1)}), bf16[192,3072]{1,0:T(8,128)(2,1)}) %all-gather.14.cloned.1.call-update) | async-done | bytes 1179664 | tf_op jit(solution)/shard_map/all_gather | solution.py:206
  691.3 50.1 %all-gather.18.cloned.1.call-done = bf16[192,6144]{1,0:T(8,128)(2,1)} async-done(((bf16[24,6144]{1,0:T(8,128)(2,1)}), bf16[192,6144]{1,0:T(8,128)(2,1)}) %all-gather.18.cloned.1.call-update) | async-done | bytes 2359312 | tf_op jit(solution)/shard_map/all_gather | solution.py:206
  (252 shorter events, 145.9 us)
Async XLA Ops:
  7.2 137.0 %copy-start = (bf16[512,768]{1,0:T(8,128)(2,1)S(1)}, bf16[512,768]{1,0:T(8,128)(2,1)}, u32[]{:S(2)}) copy-start(bf16[512,768]{1,0:T(8,128)(2,1)} %param.20) | copy-start | bytes 2359300
  7.2 106.2 %all-gather.8.cloned.1.call-start = ((), (), s32[]{:S(2)}) async-start(), calls=%async_computation.3 | async-start | bytes 4423680 | tf_op jit(solution)/shard_map/all_gather | solution.py:154
  9.5 126.0 %all-gather.10.cloned.1.call-start = ((), (), s32[]{:S(2)}) async-start(), calls=%async_computation.4 | async-start | bytes 7372800 | tf_op jit(solution)/shard_map/all_gather | solution.py:156
  14.7 147.2 %all-gather.12.cloned.1.call-start = ((), (), s32[]{:S(2)}) async-start(), calls=%async_computation.5 | async-start | bytes 11796480 | tf_op jit(solution)/shard_map/all_gather | solution.py:157
  19.7 331.3 %reduce-scatter.10.cloned.1.call-start = ((), (), s32[]{:S(2)}) async-start(), calls=%async_computation.11 | async-start | bytes 4866048 | tf_op jit(solution)/shard_map/reduce_scatter | solution.py:203
  31.1 82.2 %copy-start.50 = (f32[768]{0:T(1024)}, f32[768]{0:T(1024)S(1)}, u32[]{:S(2)}) copy-start(f32[768]{0:T(1024)S(1)} %reshape.335) | copy-start | bytes 9220
  94.5 18.3 %copy-start.55 = (s32[1,3]{1,0:T(1,128)S(1)}, s32[1,3]{1,0:T(1,128)}, u32[]{:S(2)}) copy-start(s32[1,3]{1,0:T(1,128)} %param.22) | copy-start | bytes 40
  94.5 18.4 %copy-start.30 = (bf16[512,768]{1,0:T(8,128)(2,1)S(1)}, bf16[512,768]{1,0:T(8,128)(2,1)}, u32[]{:S(2)}) copy-start(bf16[512,768]{1,0:T(8,128)(2,1)} %param.19) | copy-start | bytes 2359300
  138.3 104.4 %copy-start.6 = (f32[512,768]{1,0:T(8,128)}, f32[512,768]{1,0:T(8,128)S(1)}, u32[]{:S(2)}) copy-start(f32[512,768]{1,0:T(8,128)S(1)} %get-tuple-element.88) | copy-start | bytes 4718596
  172.4 10.2 %copy-start.42 = (bf16[512,768]{1,0:T(8,128)(2,1)S(1)}, bf16[512,768]{1,0:T(8,128)(2,1)}, u32[]{:S(2)}) copy-start(bf16[512,768]{1,0:T(8,128)(2,1)} %param.21) | copy-start | bytes 2359300
  172.4 18.7 %slice-start.6 = ((s8[9437184]{0:T(1024)(128)(4,1)}), s8[4194304]{0:T(1024)(128)(4,1)S(1)}, s32[]{:S(2)}) async-start(s8[9437184]{0:T(1024)(128)(4,1)} %bitcast.114), calls=%async_computation.18 | async-start | bytes 8388608
  203.2 16.9 %slice-start.3 = ((s8[12582912]{0:T(1024)(128)(4,1)}), s8[4194304]{0:T(1024)(128)(4,1)S(1)}, s32[]{:S(2)}) async-start(s8[12582912]{0:T(1024)(128)(4,1)} %bitcast.90), calls=%async_computation.15 | async-start | bytes 8388608
  203.2 16.9 %slice-start.4 = ((s8[12582912]{0:T(1024)(128)(4,1)}), s8[4194304]{0:T(1024)(128)(4,1)S(1)}, s32[]{:S(2)}) async-start(s8[12582912]{0:T(1024)(128)(4,1)} %bitcast.90), calls=%async_computation.16 | async-start | bytes 8388608
  242.5 220.2 %reduce-scatter.6.cloned.1.call-start = ((), (), s32[]{:S(2)}) async-start(), calls=%async_computation.6 | async-start | bytes 4866048 | tf_op jit(solution)/shard_map/reduce_scatter | solution.py:203
  257.0 12.8 %slice-start = ((s8[12582912]{0:T(1024)(128)(4,1)}), s8[4194304]{0:T(1024)(128)(4,1)S(1)}, s32[]{:S(2)}) async-start(s8[12582912]{0:T(1024)(128)(4,1)} %bitcast.88), calls=%async_computation.12 | async-start | bytes 8388608
  257.0 12.8 %slice-start.1 = ((s8[12582912]{0:T(1024)(128)(4,1)}), s8[4194304]{0:T(1024)(128)(4,1)S(1)}, s32[]{:S(2)}) async-start(s8[12582912]{0:T(1024)(128)(4,1)} %bitcast.88), calls=%async_computation.13 | async-start | bytes 8388608
  257.0 12.8 %slice-start.2 = ((s8[12582912]{0:T(1024)(128)(4,1)}), s8[4194304]{0:T(1024)(128)(4,1)S(1)}, s32[]{:S(2)}) async-start(s8[12582912]{0:T(1024)(128)(4,1)} %bitcast.88), calls=%async_computation.14 | async-start | bytes 8388608
  288.2 315.8 %reduce-scatter.8.cloned.1.call-start = ((), (), s32[]{:S(2)}) async-start(), calls=%async_computation.9 | async-start | bytes 9732096 | tf_op jit(solution)/shard_map/reduce_scatter | solution.py:203
  311.6 292.4 %copy-start.22 = (s32[512,512]{0,1:T(8,128)S(1)}, s32[512,512]{0,1:T(8,128)}, u32[]{:S(2)}) copy-start(s32[512,512]{0,1:T(8,128)} %copy-done.21) | copy-start | bytes 3145732
  311.6 359.7 %all-gather.16.cloned.1.call-start = ((), (), s32[]{:S(2)}) async-start(), calls=%async_computation.8 | async-start | bytes 1327104 | tf_op jit(solution)/shard_map/all_gather | solution.py:206
  351.0 337.6 %all-gather.14.cloned.1.call-start = ((), (), s32[]{:S(2)}) async-start(), calls=%async_computation.7 | async-start | bytes 1327104 | tf_op jit(solution)/shard_map/all_gather | solution.py:206
  462.8 278.5 %all-gather.18.cloned.1.call-start = ((), (), s32[]{:S(2)}) async-start(), calls=%async_computation.10 | async-start | bytes 2654208 | tf_op jit(solution)/shard_map/all_gather | solution.py:206
  612.6 48.6 %copy-start.49 = (f32[512]{0:T(512)S(1)}, f32[512]{0:T(512)}, u32[]{:S(2)}) copy-start(f32[512]{0:T(512)} %copy-done.48) | copy-start | bytes 6148
  612.6 48.6 %copy-start.32 = (bf16[512,768]{1,0:T(8,128)(2,1)S(1)}, bf16[512,768]{1,0:T(8,128)(2,1)}, u32[]{:S(2)}) copy-start(bf16[512,768]{1,0:T(8,128)(2,1)} %param.19) | copy-start | bytes 2359300
  (55 other events, 229.0 us)
Sparse Core Ops, SparseCore 0:
  10.2 33.7 all-gather.7
  46.1 44.1 all-gather.9
  91.8 64.2 all-gather.11
  242.7 108.2 reduce-scatter.9
  356.3 106.4 reduce-scatter.5
  468.5 135.4 reduce-scatter.7
  606.2 40.2 all-gather.15
  648.6 39.9 all-gather.13
  690.8 50.4 all-gather.17
where the time goes:
time: 762 us; the launch traced here: 754 us
  waiting for transfers between devices  357 us (47%)
  matrix products  149 us (20%)
  local copies, waits for them, and re-layouts  124 us (16%)
  other arithmetic  57.1 us (7%)
  blocking collectives  50.1 us (7%)
  between operations  15.8 us (2%)
    reduce_scatter x3, waiting for transfers between devices, reduce_rows(): lax.psum_scatter(packed.astype(jnp.bfloat16), ('fsdp', 'replica'), scatte...  292 us
    all_gather x3, waiting for transfers between devices, reduce_rows(): return lax.all_gather(owned, 'replica', axis=0, tiled=True)  64.7 us
    eq x1, local copies, waits for them, and re-layouts, block_terms(): bucket[:, :, None] == jnp.arange(BUCKETS, dtype=jnp.int32)[None, None, :]  46.2 us
    psum x1, blocking collectives, on_device(): lax.psum(jnp.concatenate([gainself_grad, gaincross_grad, gainffn_grad, re...  40.8 us
    dot_general x7, matrix products, right_product(): lax.dot_general(left, right, (((1,), (1,)), ((), ())), preferred_element_...  31.6 us
    dot_general x7, matrix products, product(): return jnp.dot(left, right, preferred_element_type=jnp.float32)  29.6 us
    dot_general x2, matrix products, attend_backward(): jnp.einsum('qhd,khd->hqk', grad_block, value_heads, preferred_element_typ...  21.8 us
    unnamed x148, local copies, waits for them, and re-layouts  21.7 us
  transfers between devices with their start and end apart: 9, of which 5 were waited for; matrix products, arithmetic and copies ran while one was open for 31% of the time, Pallas kernels for 0%

commit v1 on v0

--- a/solution.py
+++ b/solution.py
@@ -10,6 +10,32 @@
 EPS = 1e-06
 NEG = -1000000000.0
 EDGES = (1, 2, 3, 4, 5, 6, 7, 8, 12, 16, 23, 32, 46, 64, 91)
+
+
+def play_table(panel, d_out):
+    aux = jax.lax.psum(1, "replica")
+    item_now = jax.lax.axis_index("replica")
+    prior, t_next, y = (aux, item_now, panel.shape[d_out])
+    entries = [jj * prior if k0 == d_out else jj for k0, jj in enumerate(panel.shape)]
+    carry_in = lax.dynamic_update_slice_in_dim(
+        jnp.zeros(entries, panel.dtype), panel, t_next * y, axis=d_out
+    )
+    formed = finding = panel
+    for c in range(1, prior // 2 + 1):
+        formed = jax.lax.ppermute(
+            formed, "replica", list(map(lambda k0: (k0, (k0 + 1) % prior), range(prior)))
+        )
+        carry_in = lax.dynamic_update_slice_in_dim(
+            carry_in, formed, (t_next - c) % prior * y, axis=d_out
+        )
+        if 2 * c < prior:
+            finding = jax.lax.ppermute(
+                finding, "replica", list(map(lambda k0: (k0, (k0 - 1) % prior), range(prior)))
+            )
+            carry_in = lax.dynamic_update_slice_in_dim(
+                carry_in, finding, (t_next + c) % prior * y, axis=d_out
+            )
+    return carry_in
 
 
 def rms_scale(hidden, gain):
@@ -203,7 +229,7 @@
             owned = lax.psum_scatter(
                 packed.astype(jnp.bfloat16), ("fsdp", "replica"), scatter_dimension=0, tiled=True
             )
-            return lax.all_gather(owned, "replica", axis=0, tiled=True)
+            return play_table(owned, 0)
 
         downproj_grad = left_product(inner, output_grad)
         inner_grad = right_product(output_grad, down_full)

time: 762 us -> 675 us (0.89)
  waiting for transfers between devices: 357 us -> 232 us
  starting transfers between devices: 0.58 us -> 43.3 us
    reduce_scatter x3, waiting for transfers between devices: 292 us -> 173 us  [reduce_rows(): lax.psum_scatter(packed.astype(jnp.bfloat16), ('fsdp', 'replica'), scatte...]
    all_gather x3 -> x0, waiting for transfers between devices: 64.7 us -> none  [reduce_rows(): return lax.all_gather(owned, 'replica', axis=0, tiled=True)]
    ppermute x0 -> x21, waiting for transfers between devices: none -> 58.5 us  [the longest x12 47.7 us: play_table(): jax.lax.ppermute(formed, 'replica', list(map(lambda k0: (k0, (k0 + 1) % p...]
    ppermute x0 -> x21, starting transfers between devices: none -> 42.8 us  [the longest x9 26.6 us: play_table(): jax.lax.ppermute(finding, 'replica', list(map(lambda k0: (k0, (k0 - 1) %...]
    unnamed x148 -> x158, local copies, waits for them, and re-layouts: 21.7 us -> 20.6 us
  transfers between devices with their start and end apart: 9 -> 27, of which waited for: 5 -> 12; matrix products, arithmetic and copies ran while one was open for 31% -> 34% of each run, Pallas kernels for 0% -> 0%
where the time goes in v1:
time: 675 us; the launch traced here: 667 us
  waiting for transfers between devices  232 us (34%)
  matrix products  150 us (22%)
  local copies, waits for them, and re-layouts  123 us (18%)
  other arithmetic  53 us (8%)
  blocking collectives  49.1 us (7%)
  starting transfers between devices  43.3 us (6%)
  between operations  16.4 us (2%)
    reduce_scatter x3, waiting for transfers between devices, reduce_rows(): lax.psum_scatter(packed.astype(jnp.bfloat16), ('fsdp', 'replica'), scatte...  173 us
    ppermute x12, waiting for transfers between devices, play_table(): jax.lax.ppermute(formed, 'replica', list(map(lambda k0: (k0, (k0 + 1) % p...  47.7 us
    eq x1, local copies, waits for them, and re-layouts, block_terms(): bucket[:, :, None] == jnp.arange(BUCKETS, dtype=jnp.int32)[None, None, :]  45.9 us
    psum x1, blocking collectives, on_device(): lax.psum(jnp.concatenate([gainself_grad, gaincross_grad, gainffn_grad, re...  39.9 us
    dot_general x7, matrix products, right_product(): lax.dot_general(left, right, (((1,), (1,)), ((), ())), preferred_element_...  31.5 us
    dot_general x7, matrix products, product(): return jnp.dot(left, right, preferred_element_type=jnp.float32)  29.9 us
    ppermute x9, starting transfers between devices, play_table(): jax.lax.ppermute(finding, 'replica', list(map(lambda k0: (k0, (k0 - 1) %...  26.6 us
    dot_general x2, matrix products, attend_backward(): jnp.einsum('qhd,khd->hqk', grad_block, value_heads, preferred_element_typ...  21.8 us
  transfers between devices with their start and end apart: 27, of which 12 were waited for; matrix products, arithmetic and copies ran while one was open for 34% of the time, Pallas kernels for 0%

profile of v1, /device:TPU:0, one launch (start us, length us, event | category | flops | bytes accessed | tf_op | source)
XLA Modules:
  0.0 666.6 jit_solution(7170786070298802272)
XLA Ops:
  19.1 9.2 %all-reduce = bf16[2688]{0:T(1024)(128)(2,1)S(1)} all-reduce(bf16[2688]{0:T(1024)(128)(2,1)S(1)} %dynamic-update-slice), channel_id=2, replica_groups=mesh['fsdp'=4,'replica'=8] {'fsdp'}, use_global_device_ids=true, to_apply=%add | all-reduce | flops 2688 | bytes 10752
  29.5 8.7 %iota_compare_fusion = pred[512,512,32]{0,2,1:T(32,128)(4,1)} fusion(s32[512,512]{0,1:T(8,128)S(1)} %convert_add_fusion.1), kind=kLoop, calls=%fused_computation | loop fusion | flops 8388608 | bytes 9437184 | tf_op jit(solution)/shard_map/eq | solution.py:80
  38.3 45.9 %copy.127 = pred[512,512,32]{1,2,0:T(32,128)(4,1)S(1)} copy(pred[512,512,32]{0,2,1:T(32,128)(4,1)} %iota_compare_fusion) | data formatting | bytes 16777216 | tf_op jit(solution)/shard_map/eq | solution.py:80
  84.2 7.7 %fusion.83 = f32[12,512,512]{2,0,1:T(8,128)} fusion(pred[512,512,32]{1,2,0:T(32,128)(4,1)S(1)} %copy.127, bf16[32,12]{1,0:T(8,128)(2,1)S(1)} %reshape.325), kind=kOutput, calls=%fused_computation.155 | convolution fusion | flops 201326592 | bytes 20972288 | tf_op jit(solution)/shard_map/qkb,bh->hqk/dot_general | solution.py:83
  91.8 18.2 %copy.128 = f32[12,512,512]{1,2,0:T(8,128)} copy(f32[12,512,512]{2,0,1:T(8,128)} %fusion.83) | data formatting | bytes 25165824 | tf_op jit(solution)/shard_map/qkb,bh->hqk/dot_general | solution.py:83
  118.4 6.5 fusion.97
  162.8 6.6 reshape_reshape.3
  169.4 10.2 %fusion.16 = f32[512,4096]{1,0:T(8,128)} fusion(bf16[768,6144]{1,0:T(8,128)(2,1)} %all-gather.9.cloned.1.call-done, f32[512,768]{1,0:T(8,128)} %get-tuple-element.56, f32[768]{0:T(1024)S(1)} %reshape.337, f32[512]{0:T(512)S(1)} %fusion.87), kind=kOutput, calls=%fused_computation.30 | convolution fusion | flops 3222405120 | bytes 16258048 | tf_op jit(solution)/shard_map/dot_general | solution.py:50
  179.7 8.3 %fusion.24 = (bf16[512,2048]{1,0:T(8,128)(2,1)S(1)}, bf16[512,2048]{1,0:T(8,128)(2,1)S(1)}, bf16[512,2048]{1,0:T(8,128)(2,1)}) fusion(f32[512,4096]{1,0:T(8,128)} %fusion.16, bf16[2048,768]{1,0:T(8,128)(2,1)S(1)} %copy-done.28, bf16[512,768]{1,0:T(8,128)(2,1)S(1)} %copy-done.42), kind=kOutput, calls=%fused_computation.42 | convolution fusion | flops 1637875712 | bytes 18612224 | tf_op jit(solution)/shard_map/dot_general | solution.py:60
  200.1 7.9 %fusion.40 = bf16[12,64,512]{2,1,0:T(8,128)(2,1)} fusion(bf16[512,12,64]{0,2,1:T(8,128)(2,1)} %bitcast.98, f32[12,512,512]{1,2,0:T(8,128)} %copy-done.2, f32[12,512]{1,0:T(8,128)S(1)} %log_add_fusion.1), kind=kOutput, calls=%fused_computation.93 | convolution fusion | flops 409337856 | bytes 14180352 | tf_op jit(solution)/shard_map/hqk,qhd->khd/dot_general | solution.py:136
  208.0 9.0 %multiply_reduce_fusion.1 = (f32[12,512]{1,0:T(8,128)S(1)}, f32[12,512,512]{1,2,0:T(8,128)}) fusion(f32[12,512,512]{1,2,0:T(8,128)} %copy-done.2, f32[12,512]{1,0:T(8,128)S(1)} %log_add_fusion.1, bf16[512,12,64]{0,2,1:T(8,128)(2,1)S(1)} %bitcast.99, bf16[512,12,64]{0,2,1:T(8,128)(2,1)S(1)} %bitcast.109), kind=kOutput, calls=%fused_computation.5 | convolution fusion | flops 412084224 | bytes 26787840 | tf_op jit(solution)/shard_map/qhd,khd->hqk/dot_general | solution.py:124
  217.0 7.1 %multiply_convert_fusion.1 = bf16[12,512,512]{1,2,0:T(8,128)(2,1)S(1)} fusion(f32[12,512,512]{1,2,0:T(8,128)} %get-tuple-element.59, f32[12,512,512]{1,2,0:T(8,128)S(1)} %bitcast.91, f32[12,512]{1,0:T(8,128)S(1)} %get-tuple-element.58, f32[12,512]{1,0:T(8,128)S(1)} %log_add_fusion.1), kind=kLoop, calls=%fused_computation.4 | loop fusion | flops 12582912 | bytes 31506432 | tf_op jit(solution)/shard_map/convert_element_type | solution.py:128
  232.6 6.6 copy.160
  253.9 12.8 %multiply_reduce_fusion = (f32[12,512]{1,0:T(8,128)S(1)}, f32[12,512,512]{1,2,0:T(8,128)}) fusion(f32[12,512,512]{1,2,0:T(8,128)} %copy-done.1, f32[12,512]{1,0:T(8,128)S(1)} %log_add_fusion, bf16[512,12,64]{0,2,1:T(8,128)(2,1)} %bitcast.96, bf16[512,12,64]{0,2,1:T(8,128)(2,1)} %bitcast.107), kind=kOutput, calls=%fused_computation.2 | convolution fusion | flops 412084224 | bytes 26787840 | tf_op jit(solution)/shard_map/qhd,khd->hqk/dot_general | solution.py:124
  266.8 7.1 %multiply_convert_fusion = bf16[12,512,512]{1,2,0:T(8,128)(2,1)S(1)} fusion(f32[12,512,512]{1,2,0:T(8,128)} %get-tuple-element.62, f32[12,512,512]{1,2,0:T(8,128)S(1)} %bitcast.89, f32[12,512]{1,0:T(8,128)S(1)} %get-tuple-element.61, f32[12,512]{1,0:T(8,128)S(1)} %log_add_fusion), kind=kLoop, calls=%fused_computation.1 | loop fusion | flops 12582912 | bytes 31506432 | tf_op jit(solution)/shard_map/convert_element_type | solution.py:128
  291.4 6.6 reshape.332
  309.8 8.5 %fusion.48 = f32[32,12]{1,0:T(8,128)S(1)} fusion(bf16[12,512,512]{1,2,0:T(8,128)(2,1)} %copy-done.3, s32[512,512]{0,1:T(8,128)S(1)} %copy-done.22), kind=kOutput, calls=%fused_computation.101 | convolution fusion | flops 209715200 | bytes 7341568 | tf_op jit(solution)/shard_map/hqk,qkb->bh/dot_general | solution.py:140
  324.8 39.9 %psum.7 = f32[2688]{0:T(1024)S(1)} all-reduce(f32[2688]{0:T(1024)S(1)} %pad_maximum_fusion.14), channel_id=1, replica_groups=mesh['fsdp'=4,'replica'=8] {'fsdp','replica'}, use_global_device_ids=true, to_apply=%region_19.20 | all-reduce | flops 2688 | bytes 21504 | tf_op jit(solution)/shard_map/psum | solution.py:279
  381.2 77.9 %reduce-scatter.6.cloned.1.call-done = bf16[24,3072]{1,0:T(8,128)(2,1)} async-done(((bf16[768,3072]{1,0:T(8,128)(2,1)}), bf16[24,3072]{1,0:T(8,128)(2,1)}) %reduce-scatter.6.cloned.1.call-update) | async-done | bytes 147472 | tf_op jit(solution)/shard_map/reduce_scatter | solution.py:229
  504.9 95.1 %reduce-scatter.8.cloned.1.call-done = bf16[24,6144]{1,0:T(8,128)(2,1)} async-done(((bf16[768,6144]{1,0:T(8,128)(2,1)}), bf16[24,6144]{1,0:T(8,128)(2,1)}) %reduce-scatter.8.cloned.1.call-update) | async-done | bytes 294928 | tf_op jit(solution)/shard_map/reduce_scatter | solution.py:229
  603.4 10.7 %collective-permute-done.15 = bf16[24,6144]{1,0:T(8,128)(2,1)S(1)} collective-permute-done((bf16[24,6144]{1,0:T(8,128)(2,1)}, bf16[24,6144]{1,0:T(8,128)(2,1)S(1)}, u32[]{:S(2)}, u32[]{:S(2)}) %collective-permute-start.15) | collective-permute-done | bytes 294944 | tf_op jit(solution)/shard_map/ppermute | solution.py:32
  624.7 10.3 %collective-permute-done.16 = bf16[24,6144]{1,0:T(8,128)(2,1)S(1)} collective-permute-done((bf16[24,6144]{1,0:T(8,128)(2,1)S(1)}, bf16[24,6144]{1,0:T(8,128)(2,1)S(1)}, u32[]{:S(2)}, u32[]{:S(2)}) %collective-permute-start.16) | collective-permute-done | bytes 294944 | tf_op jit(solution)/shard_map/ppermute | solution.py:25
  637.5 8.2 %collective-permute-done.18 = bf16[24,6144]{1,0:T(8,128)(2,1)S(1)} collective-permute-done((bf16[24,6144]{1,0:T(8,128)(2,1)S(1)}, bf16[24,6144]{1,0:T(8,128)(2,1)S(1)}, u32[]{:S(2)}, u32[]{:S(2)}) %collective-permute-start.18) | collective-permute-done | bytes 294944 | tf_op jit(solution)/shard_map/ppermute | solution.py:25
  645.9 9.8 %collective-permute-done.20 = bf16[24,6144]{1,0:T(8,128)(2,1)S(1)} collective-permute-done((bf16[24,6144]{1,0:T(8,128)(2,1)S(1)}, bf16[24,6144]{1,0:T(8,128)(2,1)S(1)}, u32[]{:S(2)}, u32[]{:S(2)}) %collective-permute-start.20) | collective-permute-done | bytes 294944 | tf_op jit(solution)/shard_map/ppermute | solution.py:25
  (321 shorter events, 211.2 us)
Async XLA Ops:
  7.2 103.4 %all-gather.5.cloned.1.call-start = ((), (), s32[]{:S(2)}) async-start(), calls=%async_computation.3 | async-start | bytes 4423680 | tf_op jit(solution)/shard_map/all_gather | solution.py:180
  9.5 123.3 %all-gather.7.cloned.1.call-start = ((), (), s32[]{:S(2)}) async-start(), calls=%async_computation.4 | async-start | bytes 7372800 | tf_op jit(solution)/shard_map/all_gather | solution.py:182
  11.9 146.9 %all-gather.9.cloned.1.call-start = ((), (), s32[]{:S(2)}) async-start(), calls=%async_computation.5 | async-start | bytes 11796480 | tf_op jit(solution)/shard_map/all_gather | solution.py:183
  16.9 359.6 %reduce-scatter.10.cloned.1.call-start = ((), (), s32[]{:S(2)}) async-start(), calls=%async_computation.8 | async-start | bytes 4866048 | tf_op jit(solution)/shard_map/reduce_scatter | solution.py:229
  239.2 219.8 %reduce-scatter.6.cloned.1.call-start = ((), (), s32[]{:S(2)}) async-start(), calls=%async_computation.6 | async-start | bytes 4866048 | tf_op jit(solution)/shard_map/reduce_scatter | solution.py:229
  285.2 314.8 %reduce-scatter.8.cloned.1.call-start = ((), (), s32[]{:S(2)}) async-start(), calls=%async_computation.7 | async-start | bytes 9732096 | tf_op jit(solution)/shard_map/reduce_scatter | solution.py:229
  376.5 87.0 %collective-permute-start.7 = (bf16[24,3072]{1,0:T(8,128)(2,1)}, bf16[24,3072]{1,0:T(8,128)(2,1)S(1)}, u32[]{:S(2)}, u32[]{:S(2)}) collective-permute-start(bf16[24,3072]{1,0:T(8,128)(2,1)} %reduce-scatter.10.cloned.1.call-done), channel_id=1, source_target_pairs={{0,1},{1,2},{2,3},{3,4},{4,5},{5,6},{6,7},{7,0},{8,9},{9,10},{10,1... | collective-permute-start | bytes 442376 | tf_op jit(solution)/shard_map/ppermute | solution.py:25
  378.7 86.0 %collective-permute-start.8 = (bf16[24,3072]{1,0:T(8,128)(2,1)}, bf16[24,3072]{1,0:T(8,128)(2,1)S(1)}, u32[]{:S(2)}, u32[]{:S(2)}) collective-permute-start(bf16[24,3072]{1,0:T(8,128)(2,1)} %reduce-scatter.10.cloned.1.call-done), channel_id=1, source_target_pairs={{0,7},{1,0},{2,1},{3,2},{4,3},{5,4},{6,5},{7,6},{8,15},{9,8},{10,9... | collective-permute-start | bytes 442376 | tf_op jit(solution)/shard_map/ppermute | solution.py:32
  459.1 9.2 %collective-permute-start.1 = (bf16[24,3072]{1,0:T(8,128)(2,1)}, bf16[24,3072]{1,0:T(8,128)(2,1)S(1)}, u32[]{:S(2)}, u32[]{:S(2)}) collective-permute-start(bf16[24,3072]{1,0:T(8,128)(2,1)} %reduce-scatter.6.cloned.1.call-done), channel_id=1, source_target_pairs={{0,7},{1,0},{2,1},{3,2},{4,3},{5,4},{6,5},{7,6},{8,15},{9,8},{10,9... | collective-permute-start | bytes 442376 | tf_op jit(solution)/shard_map/ppermute | solution.py:32
  462.2 12.2 %collective-permute-start = (bf16[24,3072]{1,0:T(8,128)(2,1)}, bf16[24,3072]{1,0:T(8,128)(2,1)S(1)}, u32[]{:S(2)}, u32[]{:S(2)}) collective-permute-start(bf16[24,3072]{1,0:T(8,128)(2,1)} %reduce-scatter.6.cloned.1.call-done), channel_id=1, source_target_pairs={{0,1},{1,2},{2,3},{3,4},{4,5},{5,6},{6,7},{7,0},{8,9},{9,10},{10,1... | collective-permute-start | bytes 442376 | tf_op jit(solution)/shard_map/ppermute | solution.py:25
  463.5 15.0 %collective-permute-start.9 = (bf16[24,3072]{1,0:T(8,128)(2,1)S(1)}, bf16[24,3072]{1,0:T(8,128)(2,1)S(1)}, u32[]{:S(2)}, u32[]{:S(2)}) collective-permute-start(bf16[24,3072]{1,0:T(8,128)(2,1)S(1)} %collective-permute-done.7), channel_id=1, source_target_pairs={{0,1},{1,2},{2,3},{3,4},{4,5},{5,6},{6,7},{7,0},{8,9},{9,10},{10,1... | collective-permute-start | bytes 442376 | tf_op jit(solution)/shard_map/ppermute | solution.py:25
  464.8 16.4 %collective-permute-start.10 = (bf16[24,3072]{1,0:T(8,128)(2,1)S(1)}, bf16[24,3072]{1,0:T(8,128)(2,1)S(1)}, u32[]{:S(2)}, u32[]{:S(2)}) collective-permute-start(bf16[24,3072]{1,0:T(8,128)(2,1)S(1)} %collective-permute-done.8), channel_id=1, source_target_pairs={{0,7},{1,0},{2,1},{3,2},{4,3},{5,4},{6,5},{7,6},{8,15},{9,8},{10,9... | collective-permute-start | bytes 442376 | tf_op jit(solution)/shard_map/ppermute | solution.py:32
  468.3 14.9 %collective-permute-start.3 = (bf16[24,3072]{1,0:T(8,128)(2,1)S(1)}, bf16[24,3072]{1,0:T(8,128)(2,1)S(1)}, u32[]{:S(2)}, u32[]{:S(2)}) collective-permute-start(bf16[24,3072]{1,0:T(8,128)(2,1)S(1)} %collective-permute-done.1), channel_id=1, source_target_pairs={{0,7},{1,0},{2,1},{3,2},{4,3},{5,4},{6,5},{7,6},{8,15},{9,8},{10,9... | collective-permute-start | bytes 442376 | tf_op jit(solution)/shard_map/ppermute | solution.py:32
  474.4 12.0 %collective-permute-start.2 = (bf16[24,3072]{1,0:T(8,128)(2,1)S(1)}, bf16[24,3072]{1,0:T(8,128)(2,1)S(1)}, u32[]{:S(2)}, u32[]{:S(2)}) collective-permute-start(bf16[24,3072]{1,0:T(8,128)(2,1)S(1)} %collective-permute-done), channel_id=1, source_target_pairs={{0,1},{1,2},{2,3},{3,4},{4,5},{5,6},{6,7},{7,0},{8,9},{9,10},{10,1... | collective-permute-start | bytes 442376 | tf_op jit(solution)/shard_map/ppermute | solution.py:25
  478.5 11.2 %collective-permute-start.11 = (bf16[24,3072]{1,0:T(8,128)(2,1)S(1)}, bf16[24,3072]{1,0:T(8,128)(2,1)S(1)}, u32[]{:S(2)}, u32[]{:S(2)}) collective-permute-start(bf16[24,3072]{1,0:T(8,128)(2,1)S(1)} %collective-permute-done.9), channel_id=1, source_target_pairs={{0,1},{1,2},{2,3},{3,4},{4,5},{5,6},{6,7},{7,0},{8,9},{9,10},{10,1... | collective-permute-start | bytes 442376 | tf_op jit(solution)/shard_map/ppermute | solution.py:25
  481.1 14.3 %collective-permute-start.12 = (bf16[24,3072]{1,0:T(8,128)(2,1)S(1)}, bf16[24,3072]{1,0:T(8,128)(2,1)S(1)}, u32[]{:S(2)}, u32[]{:S(2)}) collective-permute-start(bf16[24,3072]{1,0:T(8,128)(2,1)S(1)} %collective-permute-done.10), channel_id=1, source_target_pairs={{0,7},{1,0},{2,1},{3,2},{4,3},{5,4},{6,5},{7,6},{8,15},{9,8},{10,9... | collective-permute-start | bytes 442376 | tf_op jit(solution)/shard_map/ppermute | solution.py:32
  483.2 12.2 %collective-permute-start.5 = (bf16[24,3072]{1,0:T(8,128)(2,1)S(1)}, bf16[24,3072]{1,0:T(8,128)(2,1)S(1)}, u32[]{:S(2)}, u32[]{:S(2)}) collective-permute-start(bf16[24,3072]{1,0:T(8,128)(2,1)S(1)} %collective-permute-done.3), channel_id=1, source_target_pairs={{0,7},{1,0},{2,1},{3,2},{4,3},{5,4},{6,5},{7,6},{8,15},{9,8},{10,9... | collective-permute-start | bytes 442376 | tf_op jit(solution)/shard_map/ppermute | solution.py:32
  489.7 9.3 %collective-permute-start.13 = (bf16[24,3072]{1,0:T(8,128)(2,1)S(1)}, bf16[24,3072]{1,0:T(8,128)(2,1)S(1)}, u32[]{:S(2)}, u32[]{:S(2)}) collective-permute-start(bf16[24,3072]{1,0:T(8,128)(2,1)S(1)} %collective-permute-done.11), channel_id=1, source_target_pairs={{0,1},{1,2},{2,3},{3,4},{4,5},{5,6},{6,7},{7,0},{8,9},{9,10},{10,1... | collective-permute-start | bytes 442376 | tf_op jit(solution)/shard_map/ppermute | solution.py:25
  600.0 14.2 %collective-permute-start.15 = (bf16[24,6144]{1,0:T(8,128)(2,1)}, bf16[24,6144]{1,0:T(8,128)(2,1)S(1)}, u32[]{:S(2)}, u32[]{:S(2)}) collective-permute-start(bf16[24,6144]{1,0:T(8,128)(2,1)} %reduce-scatter.8.cloned.1.call-done), channel_id=1, source_target_pairs={{0,7},{1,0},{2,1},{3,2},{4,3},{5,4},{6,5},{7,6},{8,15},{9,8},{10,9... | collective-permute-start | bytes 884744 | tf_op jit(solution)/shard_map/ppermute | solution.py:32
  603.1 16.7 %collective-permute-start.14 = (bf16[24,6144]{1,0:T(8,128)(2,1)}, bf16[24,6144]{1,0:T(8,128)(2,1)S(1)}, u32[]{:S(2)}, u32[]{:S(2)}) collective-permute-start(bf16[24,6144]{1,0:T(8,128)(2,1)} %reduce-scatter.8.cloned.1.call-done), channel_id=1, source_target_pairs={{0,1},{1,2},{2,3},{3,4},{4,5},{5,6},{6,7},{7,0},{8,9},{9,10},{10,1... | collective-permute-start | bytes 884744 | tf_op jit(solution)/shard_map/ppermute | solution.py:25
  619.9 15.1 %collective-permute-start.16 = (bf16[24,6144]{1,0:T(8,128)(2,1)S(1)}, bf16[24,6144]{1,0:T(8,128)(2,1)S(1)}, u32[]{:S(2)}, u32[]{:S(2)}) collective-permute-start(bf16[24,6144]{1,0:T(8,128)(2,1)S(1)} %collective-permute-done.14), channel_id=1, source_target_pairs={{0,1},{1,2},{2,3},{3,4},{4,5},{5,6},{6,7},{7,0},{8,9},{9,10},{10,1... | collective-permute-start | bytes 884744 | tf_op jit(solution)/shard_map/ppermute | solution.py:25
  622.3 23.5 %collective-permute-start.19 = (bf16[24,6144]{1,0:T(8,128)(2,1)S(1)}, bf16[24,6144]{1,0:T(8,128)(2,1)S(1)}, u32[]{:S(2)}, u32[]{:S(2)}) collective-permute-start(bf16[24,6144]{1,0:T(8,128)(2,1)S(1)} %collective-permute-done.17), channel_id=1, source_target_pairs={{0,7},{1,0},{2,1},{3,2},{4,3},{5,4},{6,5},{7,6},{8,15},{9,8},{10,9... | collective-permute-start | bytes 884744 | tf_op jit(solution)/shard_map/ppermute | solution.py:32
  635.0 10.8 %collective-permute-start.18 = (bf16[24,6144]{1,0:T(8,128)(2,1)S(1)}, bf16[24,6144]{1,0:T(8,128)(2,1)S(1)}, u32[]{:S(2)}, u32[]{:S(2)}) collective-permute-start(bf16[24,6144]{1,0:T(8,128)(2,1)S(1)} %collective-permute-done.16), channel_id=1, source_target_pairs={{0,1},{1,2},{2,3},{3,4},{4,5},{5,6},{6,7},{7,0},{8,9},{9,10},{10,1... | collective-permute-start | bytes 884744 | tf_op jit(solution)/shard_map/ppermute | solution.py:25
  645.8 9.9 %collective-permute-start.20 = (bf16[24,6144]{1,0:T(8,128)(2,1)S(1)}, bf16[24,6144]{1,0:T(8,128)(2,1)S(1)}, u32[]{:S(2)}, u32[]{:S(2)}) collective-permute-start(bf16[24,6144]{1,0:T(8,128)(2,1)S(1)} %collective-permute-done.18), channel_id=1, source_target_pairs={{0,1},{1,2},{2,3},{3,4},{4,5},{5,6},{6,7},{7,0},{8,9},{9,10},{10,1... | collective-permute-start | bytes 884744 | tf_op jit(solution)/shard_map/ppermute | solution.py:25
  (78 other events, 805.9 us)
Sparse Core Ops, SparseCore 0:
  10.2 33.7 all-gather.4
  46.1 44.1 all-gather.6
  91.8 64.2 all-gather.8
  239.4 107.8 reduce-scatter.9
  352.6 106.4 reduce-scatter.5
  464.8 135.1 reduce-scatter.7
